TPU v7x, 32 devices: a whole 2x2x4 slice. The times are simulated.
32 devices in a mesh: group: 2 (over y), ctx: 8 (over z, x), dp: 2 (over core).
Axes of the slice: x: 2, y: 2, z: 4, core: 2. Of those that a mesh axis runs over, the one named last changes fastest.
Arguments:
- queries: bfloat16 [4, 1024, 512], P(('group', 'dp'), 'ctx'), parts along dimension 0, may hold values from -30 to 30
- key_rows: bfloat16 [4, 1024, 512], P(('group', 'dp'), 'ctx'), parts along dimension 0, may hold values from -30 to 30
- values: bfloat16 [4, 1024, 512], P(('group', 'dp'), 'ctx'), parts along dimension 0, may hold values from -6 to 6
- cotangent: bfloat16 [4, 1024, 1024], P(('group', 'dp'), 'ctx'), parts along dimension 0, may hold values from -6 to 6
- out_proj: bfloat16 [512, 1024], replicated, may hold values from -6 to 6
- conv_kernel: float32 [31, 1024], replicated, may hold values from -1.8 to 1.8
- lengths: int32 [4], P(('group', 'dp')), parts along dimension 0, may hold values from 640 to 1024, as said below
Outputs:
- grad_query: bfloat16 [4, 1024, 512], P(('group', 'dp'), 'ctx'), parts along dimension 0
- grad_key: bfloat16 [4, 1024, 512], P(('group', 'dp'), 'ctx'), parts along dimension 0
- grad_value: bfloat16 [4, 1024, 512], P(('group', 'dp'), 'ctx'), parts along dimension 0
- grad_out_proj: bfloat16 [1024, 1024], P('group'), parts along dimension 0
- grad_kernel: float32 [62, 1024], P('group'), parts along dimension 0
There are 2 independent parts, one for each index of `group`. A program takes and returns all parts, laid end to end along the dimension named above; an argument that names none is the same for every part. Nothing has to cross between parts.
Inputs may be any that keep to these rules, and one draw needn't show every extreme that they name: `lengths`: in every draw at least one recording is valid over all its 1024 frames.
All inputs are finite; a program needn't handle non-finite values.
Results may differ from a plain program's by a relative error of at most 0.014.
The roundings to bfloat16 on the way count: a program that leaves them out, or rounds other values in their place, can miss the bound.
Values may be sent and summed in bfloat16 or wider, within the bound.
No kernel may reach another device: no remote copies, remote signals or barrier semaphores. Data moves between devices by JAX's collectives and lax.ppermute only.
A program may use at most 64 MiB of HBM per device.

v0:
```python
import math
import jax
import jax.numpy as jnp
from jax import lax
from jax.sharding import PartitionSpec as P

HEADS = 8
HDIM = 64
KW = 31
REACH = 3


def passed_along(block, axis, distance):
    devices = range(lax.axis_size(axis))
    route = [(i - distance, i) for i in devices if i - distance in devices]
    return lax.ppermute(block, axis, route)


def padded(cells, sides, width):
    for axis, dim in sides:
        count = lax.axis_size(axis)
        ends = count - 1
        head = lax.slice_in_dim(cells, 0, width, axis=dim)
        tail = lax.slice_in_dim(cells, cells.shape[dim] - width, cells.shape[dim], axis=dim)
        cells = jnp.concatenate(
            [
                lax.ppermute(tail, axis, [(i, (i + 1) % count) for i in range(ends)]),
                cells,
                lax.ppermute(head, axis, [((i + 1) % count, i) for i in range(ends)]),
            ],
            axis=dim,
        )
    return cells


def collect(piece_own, shifter):
    from_below = [shifter(piece_own, distance) for distance in range(REACH, 0, -1)]
    from_above = [shifter(piece_own, -distance) for distance in range(1, REACH + 1)]
    return jnp.stack(from_below + [piece_own] + from_above, axis=0)


def give_back(partials, shifter):
    total = partials[REACH]
    for offset in range(2 * REACH + 1):
        if offset != REACH:
            total = total + shifter(partials[offset], offset - REACH)
    return total


def on_device(queries, key_rows, values, cotangent, out_proj, conv_kernel, lengths):
    tokens = queries.shape[1]
    width_heads = queries.shape[2]
    channels = out_proj.shape[1]
    span_blocks = 2 * REACH + 1
    scale_factor = 1.0 / math.sqrt(HDIM)
    halo_width = (KW - 1) // 2
    block_index = lax.axis_index("ctx")
    length_here = lengths[0]
    query_here = queries[0]
    key_here = key_rows[0]
    value_here = values[0]
    cot_here = cotangent[0]
    frames = block_index * tokens + jnp.arange(tokens, dtype=jnp.int32)
    valid_rows = frames < length_here
    key_frames = (block_index - REACH) * tokens + jnp.arange(span_blocks * tokens, dtype=jnp.int32)
    valid_keys = (key_frames >= 0) & (key_frames < length_here)

    def kv_shift(piece_rows, offset_by):
        return passed_along(piece_rows, "ctx", offset_by)

    gathered = collect(jnp.stack([key_here, value_here], axis=0), kv_shift)
    key_all = gathered[:, 0].reshape(span_blocks * tokens, HEADS, HDIM)
    value_all = gathered[:, 1].reshape(span_blocks * tokens, HEADS, HDIM)
    query_heads = query_here.reshape(tokens, HEADS, HDIM)
    scores = (
        jnp.einsum("qhd,khd->hqk", query_heads, key_all, preferred_element_type=jnp.float32)
        * scale_factor
    )
    scores = jnp.where(valid_keys[None, None, :], scores, -jnp.inf)
    row_max = jnp.max(scores, axis=2, keepdims=True)
    row_total = jnp.sum(jnp.exp(scores - row_max), axis=2, keepdims=True)
    log_total = row_max + jnp.log(row_total)
    weights = jnp.exp(scores - log_total).astype(jnp.bfloat16)
    attended = jnp.einsum("hqk,khd->qhd", weights, value_all, preferred_element_type=jnp.float32)
    attended = attended.reshape(tokens, width_heads).astype(jnp.bfloat16)
    hidden = jnp.dot(attended, out_proj, preferred_element_type=jnp.float32)
    masked = jnp.where(valid_rows[:, None], hidden, 0.0).astype(jnp.bfloat16)

    def pad_time(field_rows):
        return padded(field_rows, (("ctx", 0),), halo_width)

    padded_m = pad_time(masked)
    conv_out = jnp.zeros((tokens, channels), jnp.float32)
    for tap_index in range(KW):
        conv_out = conv_out + conv_kernel[tap_index] * padded_m[tap_index : tap_index + tokens]
    sigmoid_c = jax.nn.sigmoid(conv_out)
    grad_conv = (
        cot_here.astype(jnp.float32) * (sigmoid_c + conv_out * sigmoid_c * (1.0 - sigmoid_c))
    ).astype(jnp.bfloat16)
    padded_g = pad_time(grad_conv)
    grad_wide = grad_conv.astype(jnp.float32)
    grad_masked = jnp.zeros((tokens, channels), jnp.float32)
    kernel_terms = []
    for tap_index in range(KW):
        start_row = 2 * halo_width - tap_index
        grad_masked = (
            grad_masked + conv_kernel[tap_index] * padded_g[start_row : start_row + tokens]
        )
        kernel_terms.append(
            jnp.sum(
                padded_m[tap_index : tap_index + tokens].astype(jnp.float32) * grad_wide, axis=0
            )
        )
    kernel_local = jnp.stack(kernel_terms, axis=0)
    grad_hidden = (
        cot_here.astype(jnp.float32) + jnp.where(valid_rows[:, None], grad_masked, 0.0)
    ).astype(jnp.bfloat16)
    proj_local = lax.dot_general(
        attended, grad_hidden, (((0,), (0,)), ((), ())), preferred_element_type=jnp.float32
    )
    proj_part = lax.psum_scatter(proj_local, ("ctx", "dp"), scatter_dimension=0, tiled=True)
    proj_sum = lax.all_gather(proj_part.astype(jnp.bfloat16), ("ctx", "dp"), axis=0, tiled=True)
    kernel_sum = lax.psum(kernel_local, ("ctx", "dp"))
    grad_attended = lax.dot_general(
        grad_hidden, out_proj, (((1,), (1,)), ((), ())), preferred_element_type=jnp.float32
    ).astype(jnp.bfloat16)
    grad_heads = grad_attended.reshape(tokens, HEADS, HDIM)
    attended_heads = attended.reshape(tokens, HEADS, HDIM)
    delta_rows = jnp.sum(
        grad_heads.astype(jnp.float32) * attended_heads.astype(jnp.float32), axis=2
    )
    grad_weights = jnp.einsum(
        "qhd,khd->hqk", grad_heads, value_all, preferred_element_type=jnp.float32
    )
    grad_logits = (weights.astype(jnp.float32) * (grad_weights - delta_rows.T[:, :, None])).astype(
        jnp.bfloat16
    )
    grad_query = (
        jnp.einsum("hqk,khd->qhd", grad_logits, key_all, preferred_element_type=jnp.float32)
        * scale_factor
    )
    grad_query = grad_query.reshape(tokens, width_heads).astype(jnp.bfloat16)
    grad_key_all = (
        jnp.einsum("hqk,qhd->khd", grad_logits, query_heads, preferred_element_type=jnp.float32)
        * scale_factor
    )
    grad_value_all = jnp.einsum(
        "hqk,qhd->khd", weights, grad_heads, preferred_element_type=jnp.float32
    )
    placed = jnp.stack(
        [
            grad_key_all.reshape(span_blocks, tokens, width_heads),
            grad_value_all.reshape(span_blocks, tokens, width_heads),
        ],
        axis=1,
    )

    def grad_shift(piece_rows, offset_by):
        return passed_along(piece_rows, "ctx", offset_by)

    own_grads = give_back(placed, grad_shift)
    grad_key = own_grads[0].astype(jnp.bfloat16)
    grad_value = own_grads[1].astype(jnp.bfloat16)
    return (grad_query[None], grad_key[None], grad_value[None], proj_sum, kernel_sum)


def solution(mesh):
    return jax.shard_map(
        on_device,
        mesh=mesh,
        in_specs=(
            P(("group", "dp"), "ctx", None),
            P(("group", "dp"), "ctx", None),
            P(("group", "dp"), "ctx", None),
            P(("group", "dp"), "ctx", None),
            P(),
            P(),
            P(("group", "dp")),
        ),
        out_specs=(
            P(("group", "dp"), "ctx", None),
            P(("group", "dp"), "ctx", None),
            P(("group", "dp"), "ctx", None),
            P("group", None),
            P("group", None),
        ),
        check_vma=False,
    )
```

profile of v0, /device:TPU:8, one launch (start us, length us, event | category | flops | bytes accessed | tf_op | source)
XLA Modules:
  0.0 315.7 jit_solution(5518717356108394734)
XLA Ops:
  9.1 4.4 %collective-permute-start = (bf16[2,128,512]{2,1,0:T(8,128)(2,1)S(1)}, bf16[2,128,512]{2,1,0:T(8,128)(2,1)S(1)}, u32[]{:S(2)}, u32[]{:S(2)}) collective-permute-start(bf16[2,128,512]{2,1,0:T(8,128)(2,1)S(1)} %constant_dynamic-update-slice_fusion), channel_id=1, source_target_pairs={{0,6},{2,8},{4,10},{6,12},{8,14},{1,7},{3,9},{5,11},{7,13},{9,15},... | collective-permute-start | bytes 786440 | tf_op jit(solution)/shard_map/ppermute | solution.py:16
  13.6 3.5 %collective-permute-start.1 = (bf16[2,128,512]{2,1,0:T(8,128)(2,1)S(1)}, bf16[2,128,512]{2,1,0:T(8,128)(2,1)S(1)}, u32[]{:S(2)}, u32[]{:S(2)}) collective-permute-start(bf16[2,128,512]{2,1,0:T(8,128)(2,1)S(1)} %constant_dynamic-update-slice_fusion), channel_id=1, source_target_pairs={{0,4},{2,6},{4,8},{6,10},{8,12},{10,14},{1,5},{3,7},{5,9},{7,11},{... | collective-permute-start | bytes 786440 | tf_op jit(solution)/shard_map/ppermute | solution.py:16
  19.0 4.8 %collective-permute-start.3 = (bf16[2,128,512]{2,1,0:T(8,128)(2,1)S(1)}, bf16[2,128,512]{2,1,0:T(8,128)(2,1)S(1)}, u32[]{:S(2)}, u32[]{:S(2)}) collective-permute-start(bf16[2,128,512]{2,1,0:T(8,128)(2,1)S(1)} %constant_dynamic-update-slice_fusion), channel_id=1, source_target_pairs={{2,0},{4,2},{6,4},{8,6},{10,8},{12,10},{14,12},{3,1},{5,3},{7,5},{... | collective-permute-start | bytes 786440 | tf_op jit(solution)/shard_map/ppermute | solution.py:16
  25.7 2.0 fusion.150
  32.4 7.2 %collective-permute-done.3 = bf16[2,128,512]{2,1,0:T(8,128)(2,1)S(1)} collective-permute-done((bf16[2,128,512]{2,1,0:T(8,128)(2,1)S(1)}, bf16[2,128,512]{2,1,0:T(8,128)(2,1)S(1)}, u32[]{:S(2)}, u32[]{:S(2)}) %collective-permute-start.3) | collective-permute-done | bytes 262176 | tf_op jit(solution)/shard_map/ppermute | solution.py:16
  39.6 2.6 collective-permute-done.4
  47.8 2.4 copy.27
  50.2 2.9 reshape_squeeze.11
  55.4 8.2 %collective-permute-start.7 = (bf16[15,1024]{1,0:T(8,128)(2,1)S(1)}, bf16[15,1024]{1,0:T(8,128)(2,1)S(1)}, u32[]{:S(2)}, u32[]{:S(2)}) collective-permute-start(bf16[15,1024]{1,0:T(8,128)(2,1)S(1)} %get-tuple-element.61), channel_id=1, source_target_pairs={{2,0},{4,2},{6,4},{8,6},{10,8},{12,10},{14,12},{3,1},{5,3},{7,5},{... | collective-permute-start | bytes 92168 | tf_op jit(solution)/shard_map/ppermute | solution.py:29
  66.7 3.6 %collective-permute-done.6 = bf16[15,1024]{1,0:T(8,128)(2,1)S(1)} collective-permute-done((bf16[15,1024]{1,0:T(8,128)(2,1)S(1)}, bf16[15,1024]{1,0:T(8,128)(2,1)S(1)}, u32[]{:S(2)}, u32[]{:S(2)}) %collective-permute-start.6) | collective-permute-done | bytes 30752 | tf_op jit(solution)/shard_map/ppermute | solution.py:27
  70.4 4.1 %fusion.84 = (f32[1024]{0:T(1024)}, f32[1024]{0:T(1024)}, f32[1024]{0:T(1024)}, f32[1024]{0:T(1024)}, f32[1024]{0:T(1024)}, /*index=5*/f32[1024]{0:T(1024)}, f32...) fusion(bf16[15,1024]{1,0:T(8,128)(2,1)S(1)} %collective-permute-done.7, ...), kind=kLoop, calls=%fused_computation.216 | loop fusion | flops 31841280 | bytes 1011712 | tf_op jit(solution)/shard_map/reduce_sum | solution.py:110
  76.5 4.8 %collective-permute-start.8 = (bf16[15,1024]{1,0:T(8,128)(2,1)S(1)}, bf16[15,1024]{1,0:T(8,128)(2,1)S(1)}, u32[]{:S(2)}, u32[]{:S(2)}) collective-permute-start(bf16[15,1024]{1,0:T(8,128)(2,1)S(1)} %get-tuple-element.58), channel_id=1, source_target_pairs={{2,0},{4,2},{6,4},{8,6},{10,8},{12,10},{14,12},{3,1},{5,3},{7,5},{... | collective-permute-start | bytes 92168 | tf_op jit(solution)/shard_map/ppermute | solution.py:29
  82.9 3.1 fusion.37
  91.7 2.1 multiply_convert_fusion
  95.1 2.1 multiply_bitcast_fusion
  97.1 2.8 stack_reshape.6
  99.9 2.1 convolution_bitcast_fusion
  102.0 48.2 %reduce-scatter.2.cloned.1.call-done = f32[32,1024]{1,0:T(8,128)} async-done(((f32[512,1024]{1,0:T(8,128)}), f32[32,1024]{1,0:T(8,128)}) %reduce-scatter.2.cloned.1.call-update) | async-done | bytes 131088 | tf_op jit(solution)/shard_map/reduce_scatter | solution.py:121
  151.8 3.1 constant_dynamic-update-slice_fusion.3
  158.0 15.1 %fusion.145 = (f32[1,2,128,512]{2,0,3,1:T(1,128)}, f32[1,2,128,512]{2,0,3,1:T(1,128)}, f32[1,2,128,512]{2,0,3,1:T(1,128)}, f32[1,2,128,512]{2,0,3,1:T(1,128)}, f...) fusion(f32[7,2,128,512]{2,0,3,1:T(8,128)} %constant_dynamic-update-slice_fusion.2), kind=kLoop, calls=%fused_computation.316 | loop fusion | bytes 7340032 | tf_op jit(solution)/shard_map/slice | solution.py:46
  173.2 3.6 %collective-permute-start.15 = (f32[2,128,512]{1,2,0:T(8,128)S(1)}, f32[2,128,512]{1,2,0:T(8,128)S(1)}, u32[]{:S(2)}, u32[]{:S(2)}) collective-permute-start(f32[2,128,512]{1,2,0:T(8,128)S(1)} %bitcast.163), channel_id=1, source_target_pairs={{0,6},{2,8},{4,10},{6,12},{8,14},{1,7},{3,9},{5,11},{7,13},{9,15},... | collective-permute-start | bytes 1572872 | tf_op jit(solution)/shard_map/ppermute | solution.py:16
  178.1 2.4 collective-permute-start.14
  180.5 2.9 collective-permute-start.13
  183.4 4.2 %collective-permute-start.12 = (f32[2,128,512]{1,2,0:T(8,128)}, f32[2,128,512]{1,2,0:T(8,128)}, u32[]{:S(2)}, u32[]{:S(2)}) collective-permute-start(f32[2,128,512]{1,2,0:T(8,128)} %bitcast.54), channel_id=1, source_target_pairs={{2,0},{4,2},{6,4},{8,6},{10,8},{12,10},{14,12},{3,1},{5,3},{7,5},{... | collective-permute-start | bytes 1572872 | tf_op jit(solution)/shard_map/ppermute | solution.py:16
  187.6 2.6 collective-permute-start.11
  190.2 4.4 %collective-permute-done.15 = f32[2,128,512]{1,2,0:T(8,128)S(1)} collective-permute-done((f32[2,128,512]{1,2,0:T(8,128)S(1)}, f32[2,128,512]{1,2,0:T(8,128)S(1)}, u32[]{:S(2)}, u32[]{:S(2)}) %collective-permute-start.15) | collective-permute-done | bytes 524320 | tf_op jit(solution)/shard_map/ppermute | solution.py:16
  196.6 2.7 stack.167
  201.7 3.7 %collective-permute-done.14 = f32[2,128,512]{1,2,0:T(8,128)} collective-permute-done((f32[2,128,512]{1,2,0:T(8,128)}, f32[2,128,512]{1,2,0:T(8,128)}, u32[]{:S(2)}, u32[]{:S(2)}) %collective-permute-start.14) | collective-permute-done | bytes 524320 | tf_op jit(solution)/shard_map/ppermute | solution.py:16
  205.4 17.0 %collective-permute-done.13 = f32[2,128,512]{1,2,0:T(8,128)} collective-permute-done((f32[2,128,512]{1,2,0:T(8,128)}, f32[2,128,512]{1,2,0:T(8,128)}, u32[]{:S(2)}, u32[]{:S(2)}) %collective-permute-start.13) | collective-permute-done | bytes 524320 | tf_op jit(solution)/shard_map/ppermute | solution.py:16
  222.4 5.2 %collective-permute-done.11 = f32[2,128,512]{1,2,0:T(8,128)} collective-permute-done((f32[2,128,512]{1,2,0:T(8,128)}, f32[2,128,512]{1,2,0:T(8,128)}, u32[]{:S(2)}, u32[]{:S(2)}) %collective-permute-start.11) | collective-permute-done | bytes 524320 | tf_op jit(solution)/shard_map/ppermute | solution.py:16
  231.1 75.1 %all-reduce.2.cloned.1.call-done = f32[31,1024]{1,0:T(8,128)} async-done(((f32[31,1024]{1,0:T(8,128)}), f32[31,1024]{1,0:T(8,128)}) %all-reduce.2.cloned.1.call-update) | async-done | bytes 126992 | tf_op jit(solution)/shard_map/psum | solution.py:123
  306.2 2.3 copy.65
  (149 shorter events, 45.1 us)
Async XLA Ops:
  7.2 47.8 %copy-start = (bf16[512,1024]{1,0:T(8,128)(2,1)S(1)}, bf16[512,1024]{1,0:T(8,128)(2,1)}, u32[]{:S(2)}) copy-start(bf16[512,1024]{1,0:T(8,128)(2,1)} %param.11) | copy-start | bytes 3145732
  7.2 143.1 %reduce-scatter.2.cloned.1.call-start = ((), (), s32[]{:S(2)}) async-start(), calls=%async_computation.1 | async-start | bytes 2228224 | tf_op jit(solution)/shard_map/reduce_scatter | solution.py:121
  9.1 20.4 %collective-permute-start = (bf16[2,128,512]{2,1,0:T(8,128)(2,1)S(1)}, bf16[2,128,512]{2,1,0:T(8,128)(2,1)S(1)}, u32[]{:S(2)}, u32[]{:S(2)}) collective-permute-start(bf16[2,128,512]{2,1,0:T(8,128)(2,1)S(1)} %constant_dynamic-update-slice_fusion), channel_id=1, source_target_pairs={{0,6},{2,8},{4,10},{6,12},{8,14},{1,7},{3,9},{5,11},{7,13},{9,15},... | collective-permute-start | bytes 786440 | tf_op jit(solution)/shard_map/ppermute | solution.py:16
  13.6 17.3 %collective-permute-start.1 = (bf16[2,128,512]{2,1,0:T(8,128)(2,1)S(1)}, bf16[2,128,512]{2,1,0:T(8,128)(2,1)S(1)}, u32[]{:S(2)}, u32[]{:S(2)}) collective-permute-start(bf16[2,128,512]{2,1,0:T(8,128)(2,1)S(1)} %constant_dynamic-update-slice_fusion), channel_id=1, source_target_pairs={{0,4},{2,6},{4,8},{6,10},{8,12},{10,14},{1,5},{3,7},{5,9},{7,11},{... | collective-permute-start | bytes 786440 | tf_op jit(solution)/shard_map/ppermute | solution.py:16
  17.1 15.3 %collective-permute-start.2 = (bf16[2,128,512]{2,1,0:T(8,128)(2,1)S(1)}, bf16[2,128,512]{2,1,0:T(8,128)(2,1)S(1)}, u32[]{:S(2)}, u32[]{:S(2)}) collective-permute-start(bf16[2,128,512]{2,1,0:T(8,128)(2,1)S(1)} %constant_dynamic-update-slice_fusion), channel_id=1, source_target_pairs={{0,2},{2,4},{4,6},{6,8},{8,10},{10,12},{12,14},{1,3},{3,5},{5,7},{... | collective-permute-start | bytes 786440 | tf_op jit(solution)/shard_map/ppermute | solution.py:16
  19.0 20.6 %collective-permute-start.3 = (bf16[2,128,512]{2,1,0:T(8,128)(2,1)S(1)}, bf16[2,128,512]{2,1,0:T(8,128)(2,1)S(1)}, u32[]{:S(2)}, u32[]{:S(2)}) collective-permute-start(bf16[2,128,512]{2,1,0:T(8,128)(2,1)S(1)} %constant_dynamic-update-slice_fusion), channel_id=1, source_target_pairs={{2,0},{4,2},{6,4},{8,6},{10,8},{12,10},{14,12},{3,1},{5,3},{7,5},{... | collective-permute-start | bytes 786440 | tf_op jit(solution)/shard_map/ppermute | solution.py:16
  23.8 18.4 %collective-permute-start.4 = (bf16[2,128,512]{2,1,0:T(8,128)(2,1)S(1)}, bf16[2,128,512]{2,1,0:T(8,128)(2,1)S(1)}, u32[]{:S(2)}, u32[]{:S(2)}) collective-permute-start(bf16[2,128,512]{2,1,0:T(8,128)(2,1)S(1)} %constant_dynamic-update-slice_fusion), channel_id=1, source_target_pairs={{4,0},{6,2},{8,4},{10,6},{12,8},{14,10},{5,1},{7,3},{9,5},{11,7},{... | collective-permute-start | bytes 786440 | tf_op jit(solution)/shard_map/ppermute | solution.py:16
  28.4 26.5 %copy-start.42 = (pred[128]{0:T(512)(128)(4,1)}, pred[128]{0:T(512)(128)(4,1)S(1)}, u32[]{:S(2)}) copy-start(pred[128]{0:T(512)(128)(4,1)S(1)} %add_compare_fusion) | copy-start | bytes 388
  29.5 12.7 %collective-permute-start.5 = (bf16[2,128,512]{2,1,0:T(8,128)(2,1)S(1)}, bf16[2,128,512]{2,1,0:T(8,128)(2,1)S(1)}, u32[]{:S(2)}, u32[]{:S(2)}) collective-permute-start(bf16[2,128,512]{2,1,0:T(8,128)(2,1)S(1)} %constant_dynamic-update-slice_fusion), channel_id=1, source_target_pairs={{6,0},{8,2},{10,4},{12,6},{14,8},{7,1},{9,3},{11,5},{13,7},{15,9},... | collective-permute-start | bytes 786440 | tf_op jit(solution)/shard_map/ppermute | solution.py:16
  55.3 33.2 %copy-start.4 = (bf16[128,1024]{1,0:T(8,128)(2,1)}, bf16[128,1024]{1,0:T(8,128)(2,1)S(1)}, u32[]{:S(2)}) copy-start(bf16[128,1024]{1,0:T(8,128)(2,1)S(1)} %fusion.4) | copy-start | bytes 786436
  55.4 11.3 %collective-permute-start.7 = (bf16[15,1024]{1,0:T(8,128)(2,1)S(1)}, bf16[15,1024]{1,0:T(8,128)(2,1)S(1)}, u32[]{:S(2)}, u32[]{:S(2)}) collective-permute-start(bf16[15,1024]{1,0:T(8,128)(2,1)S(1)} %get-tuple-element.61), channel_id=1, source_target_pairs={{2,0},{4,2},{6,4},{8,6},{10,8},{12,10},{14,12},{3,1},{5,3},{7,5},{... | collective-permute-start | bytes 92168 | tf_op jit(solution)/shard_map/ppermute | solution.py:29
  63.6 6.7 %collective-permute-start.6 = (bf16[15,1024]{1,0:T(8,128)(2,1)S(1)}, bf16[15,1024]{1,0:T(8,128)(2,1)S(1)}, u32[]{:S(2)}, u32[]{:S(2)}) collective-permute-start(bf16[15,1024]{1,0:T(8,128)(2,1)S(1)} %get-tuple-element.60), channel_id=1, source_target_pairs={{0,2},{2,4},{4,6},{6,8},{8,10},{10,12},{12,14},{1,3},{3,5},{5,7},{... | collective-permute-start | bytes 92168 | tf_op jit(solution)/shard_map/ppermute | solution.py:27
  74.6 6.8 %collective-permute-start.9 = (bf16[15,1024]{1,0:T(8,128)(2,1)S(1)}, bf16[15,1024]{1,0:T(8,128)(2,1)S(1)}, u32[]{:S(2)}, u32[]{:S(2)}) collective-permute-start(bf16[15,1024]{1,0:T(8,128)(2,1)S(1)} %get-tuple-element.59), channel_id=1, source_target_pairs={{0,2},{2,4},{4,6},{6,8},{8,10},{10,12},{12,14},{1,3},{3,5},{5,7},{... | collective-permute-start | bytes 92168 | tf_op jit(solution)/shard_map/ppermute | solution.py:27
  76.5 6.4 %collective-permute-start.8 = (bf16[15,1024]{1,0:T(8,128)(2,1)S(1)}, bf16[15,1024]{1,0:T(8,128)(2,1)S(1)}, u32[]{:S(2)}, u32[]{:S(2)}) collective-permute-start(bf16[15,1024]{1,0:T(8,128)(2,1)S(1)} %get-tuple-element.58), channel_id=1, source_target_pairs={{2,0},{4,2},{6,4},{8,6},{10,8},{12,10},{14,12},{3,1},{5,3},{7,5},{... | collective-permute-start | bytes 92168 | tf_op jit(solution)/shard_map/ppermute | solution.py:29
  88.5 142.6 %all-gather.2.cloned.1.call-start = ((), (), s32[]{:S(2)}) async-start(), calls=%async_computation.2 | async-start | bytes 1114112 | tf_op jit(solution)/shard_map/all_gather | solution.py:122
  151.8 154.4 %all-reduce.2.cloned.1.call-start = ((), (), s32[]{:S(2)}) async-start(), calls=%async_computation.3 | async-start | bytes 262144 | tf_op jit(solution)/shard_map/psum | solution.py:123
  173.1 23.4 %copy-start.34 = (f32[1024]{0:T(1024)S(1)}, f32[1024]{0:T(1024)}, u32[]{:S(2)}) copy-start(f32[1024]{0:T(1024)} %get-tuple-element.16) | copy-start | bytes 12292
  173.1 23.4 %copy-start.35 = (f32[1024]{0:T(1024)S(1)}, f32[1024]{0:T(1024)}, u32[]{:S(2)}) copy-start(f32[1024]{0:T(1024)} %get-tuple-element.17) | copy-start | bytes 12292
  173.1 23.4 %copy-start.36 = (f32[1024]{0:T(1024)S(1)}, f32[1024]{0:T(1024)}, u32[]{:S(2)}) copy-start(f32[1024]{0:T(1024)} %get-tuple-element.18) | copy-start | bytes 12292
  173.1 23.4 %copy-start.37 = (f32[1024]{0:T(1024)S(1)}, f32[1024]{0:T(1024)}, u32[]{:S(2)}) copy-start(f32[1024]{0:T(1024)} %get-tuple-element.19) | copy-start | bytes 12292
  173.1 23.4 %copy-start.38 = (f32[1024]{0:T(1024)S(1)}, f32[1024]{0:T(1024)}, u32[]{:S(2)}) copy-start(f32[1024]{0:T(1024)} %get-tuple-element.20) | copy-start | bytes 12292
  173.1 23.4 %copy-start.39 = (f32[1024]{0:T(1024)S(1)}, f32[1024]{0:T(1024)}, u32[]{:S(2)}) copy-start(f32[1024]{0:T(1024)} %get-tuple-element.21) | copy-start | bytes 12292
  173.2 23.4 %copy-start.40 = (f32[1024]{0:T(1024)S(1)}, f32[1024]{0:T(1024)}, u32[]{:S(2)}) copy-start(f32[1024]{0:T(1024)} %get-tuple-element.22) | copy-start | bytes 12292
  173.2 23.4 %copy-start.41 = (f32[1024]{0:T(1024)S(1)}, f32[1024]{0:T(1024)}, u32[]{:S(2)}) copy-start(f32[1024]{0:T(1024)} %get-tuple-element.23) | copy-start | bytes 12292
  173.2 26.1 %copy-start.2 = (bf16[8,128,896]{1,2,0:T(8,128)(2,1)S(1)}, bf16[8,128,896]{1,2,0:T(8,128)(2,1)}, u32[]{:S(2)}) copy-start(bf16[8,128,896]{1,2,0:T(8,128)(2,1)} %copy-done.1) | copy-start | bytes 5505028
  173.2 21.5 %collective-permute-start.15 = (f32[2,128,512]{1,2,0:T(8,128)S(1)}, f32[2,128,512]{1,2,0:T(8,128)S(1)}, u32[]{:S(2)}, u32[]{:S(2)}) collective-permute-start(f32[2,128,512]{1,2,0:T(8,128)S(1)} %bitcast.163), channel_id=1, source_target_pairs={{0,6},{2,8},{4,10},{6,12},{8,14},{1,7},{3,9},{5,11},{7,13},{9,15},... | collective-permute-start | bytes 1572872 | tf_op jit(solution)/shard_map/ppermute | solution.py:16
  178.1 27.3 %collective-permute-start.14 = (f32[2,128,512]{1,2,0:T(8,128)}, f32[2,128,512]{1,2,0:T(8,128)}, u32[]{:S(2)}, u32[]{:S(2)}) collective-permute-start(f32[2,128,512]{1,2,0:T(8,128)} %bitcast.56), channel_id=1, source_target_pairs={{0,4},{2,6},{4,8},{6,10},{8,12},{10,14},{1,5},{3,7},{5,9},{7,11},{... | collective-permute-start | bytes 1572872 | tf_op jit(solution)/shard_map/ppermute | solution.py:16
  180.5 41.9 %collective-permute-start.13 = (f32[2,128,512]{1,2,0:T(8,128)}, f32[2,128,512]{1,2,0:T(8,128)}, u32[]{:S(2)}, u32[]{:S(2)}) collective-permute-start(f32[2,128,512]{1,2,0:T(8,128)} %bitcast.55), channel_id=1, source_target_pairs={{0,2},{2,4},{4,6},{6,8},{8,10},{10,12},{12,14},{1,3},{3,5},{5,7},{... | collective-permute-start | bytes 1572872 | tf_op jit(solution)/shard_map/ppermute | solution.py:16
  183.4 38.9 %collective-permute-start.12 = (f32[2,128,512]{1,2,0:T(8,128)}, f32[2,128,512]{1,2,0:T(8,128)}, u32[]{:S(2)}, u32[]{:S(2)}) collective-permute-start(f32[2,128,512]{1,2,0:T(8,128)} %bitcast.54), channel_id=1, source_target_pairs={{2,0},{4,2},{6,4},{8,6},{10,8},{12,10},{14,12},{3,1},{5,3},{7,5},{... | collective-permute-start | bytes 1572872 | tf_op jit(solution)/shard_map/ppermute | solution.py:16
  187.6 40.0 %collective-permute-start.11 = (f32[2,128,512]{1,2,0:T(8,128)}, f32[2,128,512]{1,2,0:T(8,128)}, u32[]{:S(2)}, u32[]{:S(2)}) collective-permute-start(f32[2,128,512]{1,2,0:T(8,128)} %bitcast.53), channel_id=1, source_target_pairs={{4,0},{6,2},{8,4},{10,6},{12,8},{14,10},{5,1},{7,3},{9,5},{11,7},{... | collective-permute-start | bytes 1572872 | tf_op jit(solution)/shard_map/ppermute | solution.py:16
  194.7 32.9 %collective-permute-start.10 = (f32[2,128,512]{1,2,0:T(8,128)}, f32[2,128,512]{1,2,0:T(8,128)}, u32[]{:S(2)}, u32[]{:S(2)}) collective-permute-start(f32[2,128,512]{1,2,0:T(8,128)} %bitcast.52), channel_id=1, source_target_pairs={{6,0},{8,2},{10,4},{12,6},{14,8},{7,1},{9,3},{11,5},{13,7},{15,9},... | collective-permute-start | bytes 1572872 | tf_op jit(solution)/shard_map/ppermute | solution.py:16
  196.5 31.1 %copy-start.8 = (f32[1,2,128,512]{2,0,3,1:T(1,128)S(1)}, f32[1,2,128,512]{2,0,3,1:T(1,128)}, u32[]{:S(2)}) copy-start(f32[1,2,128,512]{2,0,3,1:T(1,128)} %get-tuple-element.51) | copy-start | bytes 1572868
  (30 other events, 417.0 us)
Sparse Core Ops, SparseCore 0:
  88.7 61.5 reduce-scatter.1
  152.4 39.2 all-gather.1
  199.4 106.7 all-reduce.1
where the time goes:
time: 317 us; the launch traced here: 316 us
  waiting for transfers between devices  170 us (54%)
  starting transfers between devices  52 us (16%)
  local copies, waits for them, and re-layouts  50.2 us (16%)
  between operations  15.3 us (5%)
  other arithmetic  14.2 us (4%)
  matrix products  13.9 us (4%)
    psum x1, waiting for transfers between devices, on_device(): kernel_sum = lax.psum(kernel_local, ('ctx', 'dp'))  75.1 us
    reduce_scatter x1, waiting for transfers between devices, on_device(): lax.psum_scatter(proj_local, ('ctx', 'dp'), scatter_dimension=0, tiled=True)  48.2 us
    ppermute x12, waiting for transfers between devices, passed_along(): return lax.ppermute(block, axis, route)  41.6 us
    ppermute x12, starting transfers between devices, passed_along(): return lax.ppermute(block, axis, route)  34.9 us
    slice x1, local copies, waits for them, and re-layouts, give_back(): total = total + shifter(partials[offset], offset - REACH)  15.1 us
    unnamed x100, local copies, waits for them, and re-layouts  13.3 us
    ppermute x2, starting transfers between devices, padded(): lax.ppermute(head, axis, [((i + 1) % count, i) for i in range(ends)])  13 us
  transfers between devices with their start and end apart: 19, of which 11 were waited for; matrix products, arithmetic and copies ran while one was open for 15% of the time, Pallas kernels for 0%

commit v1 on v0

--- a/solution.py
+++ b/solution.py
@@ -120,7 +120,7 @@
     )
     proj_part = lax.psum_scatter(proj_local, ("ctx", "dp"), scatter_dimension=0, tiled=True)
     proj_sum = lax.all_gather(proj_part.astype(jnp.bfloat16), ("ctx", "dp"), axis=0, tiled=True)
-    kernel_sum = lax.psum(kernel_local, ("ctx", "dp"))
+    kernel_sum = jnp.sum(lax.all_gather(kernel_local, ("ctx", "dp")), axis=0)
     grad_attended = lax.dot_general(
         grad_hidden, out_proj, (((1,), (1,)), ((), ())), preferred_element_type=jnp.float32
     ).astype(jnp.bfloat16)

time: 317 us -> 270 us (0.85)
  waiting for transfers between devices: 170 us -> 113 us
  other arithmetic: 14.2 us -> 21.4 us
    psum x1 -> x0, waiting for transfers between devices: 75.1 us -> none  [on_device(): kernel_sum = lax.psum(kernel_local, ('ctx', 'dp'))]
    all_gather x1, waiting for transfers between devices: 0.01 us -> 29.4 us  [on_device(): lax.all_gather(proj_part.astype(jnp.bfloat16), ('ctx', 'dp'), axis=0, til...]
    reduce_scatter x1, waiting for transfers between devices: 48.2 us -> 30.6 us  [on_device(): lax.psum_scatter(proj_local, ('ctx', 'dp'), scatter_dimension=0, tiled=True)]
    ppermute x12, waiting for transfers between devices: 41.6 us -> 47.8 us  [passed_along(): return lax.ppermute(block, axis, route)]
    reduce_sum x4, other arithmetic: 5.85 us -> 10.7 us  [on_device(): jnp.sum(padded_m[tap_index:tap_index + tokens].astype(jnp.float32) * grad...]
    unnamed x100 -> x81, local copies, waits for them, and re-layouts: 13.3 us -> 11.2 us
  transfers between devices with their start and end apart: 19 -> 19, of which waited for: 11 -> 11; matrix products, arithmetic and copies ran while one was open for 15% -> 22% of each run, Pallas kernels for 0% -> 0%
where the time goes in v1:
time: 270 us; the launch traced here: 266 us
  waiting for transfers between devices  113 us (42%)
  starting transfers between devices  52 us (19%)
  local copies, waits for them, and re-layouts  51.3 us (19%)
  other arithmetic  21.4 us (8%)
  between operations  15.1 us (6%)
  matrix products  13 us (5%)
    ppermute x12, waiting for transfers between devices, passed_along(): return lax.ppermute(block, axis, route)  47.8 us
    ppermute x12, starting transfers between devices, passed_along(): return lax.ppermute(block, axis, route)  34.8 us
    reduce_scatter x1, waiting for transfers between devices, on_device(): lax.psum_scatter(proj_local, ('ctx', 'dp'), scatter_dimension=0, tiled=True)  30.6 us
    all_gather x1, waiting for transfers between devices, on_device(): lax.all_gather(proj_part.astype(jnp.bfloat16), ('ctx', 'dp'), axis=0, til...  29.4 us
    slice x1, local copies, waits for them, and re-layouts, give_back(): total = total + shifter(partials[offset], offset - REACH)  15.1 us
    ppermute x2, starting transfers between devices, padded(): lax.ppermute(head, axis, [((i + 1) % count, i) for i in range(ends)])  13 us
    unnamed x81, local copies, waits for them, and re-layouts  11.2 us
    reduce_sum x4, other arithmetic, on_device(): jnp.sum(padded_m[tap_index:tap_index + tokens].astype(jnp.float32) * grad...  10.7 us
  transfers between devices with their start and end apart: 19, of which 11 were waited for; matrix products, arithmetic and copies ran while one was open for 22% of the time, Pallas kernels for 0%

profile of v1, /device:TPU:8, one launch (start us, length us, event | category | flops | bytes accessed | tf_op | source)
XLA Modules:
  0.0 265.9 jit_solution(17418342943907672649)
XLA Ops:
  9.1 4.4 %collective-permute-start = (bf16[2,128,512]{2,1,0:T(8,128)(2,1)S(1)}, bf16[2,128,512]{2,1,0:T(8,128)(2,1)S(1)}, u32[]{:S(2)}, u32[]{:S(2)}) collective-permute-start(bf16[2,128,512]{2,1,0:T(8,128)(2,1)S(1)} %constant_dynamic-update-slice_fusion), channel_id=1, source_target_pairs={{0,6},{2,8},{4,10},{6,12},{8,14},{1,7},{3,9},{5,11},{7,13},{9,15},... | collective-permute-start | bytes 786440 | tf_op jit(solution)/shard_map/ppermute | solution.py:16
  13.6 3.5 %collective-permute-start.1 = (bf16[2,128,512]{2,1,0:T(8,128)(2,1)S(1)}, bf16[2,128,512]{2,1,0:T(8,128)(2,1)S(1)}, u32[]{:S(2)}, u32[]{:S(2)}) collective-permute-start(bf16[2,128,512]{2,1,0:T(8,128)(2,1)S(1)} %constant_dynamic-update-slice_fusion), channel_id=1, source_target_pairs={{0,4},{2,6},{4,8},{6,10},{8,12},{10,14},{1,5},{3,7},{5,9},{7,11},{... | collective-permute-start | bytes 786440 | tf_op jit(solution)/shard_map/ppermute | solution.py:16
  19.0 4.8 %collective-permute-start.3 = (bf16[2,128,512]{2,1,0:T(8,128)(2,1)S(1)}, bf16[2,128,512]{2,1,0:T(8,128)(2,1)S(1)}, u32[]{:S(2)}, u32[]{:S(2)}) collective-permute-start(bf16[2,128,512]{2,1,0:T(8,128)(2,1)S(1)} %constant_dynamic-update-slice_fusion), channel_id=1, source_target_pairs={{2,0},{4,2},{6,4},{8,6},{10,8},{12,10},{14,12},{3,1},{5,3},{7,5},{... | collective-permute-start | bytes 786440 | tf_op jit(solution)/shard_map/ppermute | solution.py:16
  34.0 8.2 %collective-permute-done.4 = bf16[2,128,512]{2,1,0:T(8,128)(2,1)S(1)} collective-permute-done((bf16[2,128,512]{2,1,0:T(8,128)(2,1)S(1)}, bf16[2,128,512]{2,1,0:T(8,128)(2,1)S(1)}, u32[]{:S(2)}, u32[]{:S(2)}) %collective-permute-start.4) | collective-permute-done | bytes 262176 | tf_op jit(solution)/shard_map/ppermute | solution.py:16
  47.8 2.4 copy.45
  50.2 3.0 %reshape_squeeze.11 = bf16[896,8,64]{0,2,1:T(8,128)(2,1)} reshape(bf16[7,1,128,512]{2,0,3,1:T(8,128)(2,1)} %copy.45) | data formatting | bytes 1835008 | tf_op jit(solution)/shard_map/reshape;squeeze | solution.py:73
  55.4 8.2 %collective-permute-start.7 = (bf16[15,1024]{1,0:T(8,128)(2,1)S(1)}, bf16[15,1024]{1,0:T(8,128)(2,1)S(1)}, u32[]{:S(2)}, u32[]{:S(2)}) collective-permute-start(bf16[15,1024]{1,0:T(8,128)(2,1)S(1)} %get-tuple-element.66), channel_id=1, source_target_pairs={{2,0},{4,2},{6,4},{8,6},{10,8},{12,10},{14,12},{3,1},{5,3},{7,5},{... | collective-permute-start | bytes 92168 | tf_op jit(solution)/shard_map/ppermute | solution.py:29
  66.7 3.6 %collective-permute-done.6 = bf16[15,1024]{1,0:T(8,128)(2,1)S(1)} collective-permute-done((bf16[15,1024]{1,0:T(8,128)(2,1)S(1)}, bf16[15,1024]{1,0:T(8,128)(2,1)S(1)}, u32[]{:S(2)}, u32[]{:S(2)}) %collective-permute-start.6) | collective-permute-done | bytes 30752 | tf_op jit(solution)/shard_map/ppermute | solution.py:27
  70.5 4.1 %fusion.84 = (f32[1024]{0:T(1024)}, f32[1024]{0:T(1024)}, f32[1024]{0:T(1024)}, f32[1024]{0:T(1024)}, f32[1024]{0:T(1024)}, /*index=5*/f32[1024]{0:T(1024)}, f32...) fusion(bf16[15,1024]{1,0:T(8,128)(2,1)S(1)} %collective-permute-done.7, ...), kind=kLoop, calls=%fused_computation.216 | loop fusion | flops 31841280 | bytes 1011712 | tf_op jit(solution)/shard_map/reduce_sum | solution.py:110
  76.5 4.8 %collective-permute-start.8 = (bf16[15,1024]{1,0:T(8,128)(2,1)S(1)}, bf16[15,1024]{1,0:T(8,128)(2,1)S(1)}, u32[]{:S(2)}, u32[]{:S(2)}) collective-permute-start(bf16[15,1024]{1,0:T(8,128)(2,1)S(1)} %get-tuple-element.63), channel_id=1, source_target_pairs={{2,0},{4,2},{6,4},{8,6},{10,8},{12,10},{14,12},{3,1},{5,3},{7,5},{... | collective-permute-start | bytes 92168 | tf_op jit(solution)/shard_map/ppermute | solution.py:29
  82.9 2.5 fusion.37
  88.2 2.1 fusion.67
  90.3 2.2 fusion.83
  92.5 2.4 fusion.68
  94.9 5.5 %stack.167 = f32[31,1024]{1,0:T(8,128)} concatenate(f32[1,1024]{1,0:T(1,128)} %bitcast.243, f32[1,1024]{1,0:T(1,128)} %bitcast.245, f32[1,1024]{1,0:T(1,128)} %bitcast.244, f32[1,1024]{1,0:T(1,128)} %bitcast.246, f32[1,1024]{1,0:T(1,128)} %bitcast.255, f32[1,1024]{1,0:T(1,128)} %bitcast.256, f32[1,1024]{1,0:T(1,128)} %bitcast.257, f32[1,1024]{1,0:T(1,128)} %bitcast.258, ...), dimensions={0} | concatenate | bytes 253952 | tf_op jit(solution)/shard_map/stack | solution.py:114
  102.0 2.1 multiply_convert_fusion
  107.5 2.7 %stack_reshape.6 = f32[7,1,128,512]{2,0,3,1:T(8,128)} reshape(f32[896,8,64]{0,2,1:T(8,128)} %multiply_bitcast_fusion) | data formatting | bytes 3670016 | tf_op jit(solution)/shard_map/stack;reshape | solution.py:150
  112.3 2.9 %stack_reshape.7 = f32[7,1,128,512]{2,0,3,1:T(8,128)} reshape(f32[896,8,64]{0,2,1:T(8,128)} %convolution_bitcast_fusion) | data formatting | bytes 3670016 | tf_op jit(solution)/shard_map/stack;reshape | solution.py:150
  119.1 30.6 %reduce-scatter.2.cloned.1.call-done = f32[32,1024]{1,0:T(8,128)} async-done(((f32[512,1024]{1,0:T(8,128)}), f32[32,1024]{1,0:T(8,128)}) %reduce-scatter.2.cloned.1.call-update) | async-done | bytes 131088 | tf_op jit(solution)/shard_map/reduce_scatter | solution.py:121
  151.3 15.1 %fusion.145 = (f32[1,2,128,512]{2,0,3,1:T(1,128)S(1)}, f32[1,2,128,512]{2,0,3,1:T(1,128)}, f32[1,2,128,512]{2,0,3,1:T(1,128)S(1)}, f32[1,2,128,512]{2,0,3,1:T(1,...) fusion(f32[7,2,128,512]{2,0,3,1:T(8,128)} %constant_dynamic-update-slice_fu, ...), kind=kLoop, calls=%fused_computation.316 | loop fusion | bytes 7340032 | tf_op jit(solution)/shard_map/slice | solution.py:46
  166.4 3.5 %collective-permute-start.15 = (f32[2,128,512]{1,2,0:T(8,128)S(1)}, f32[2,128,512]{1,2,0:T(8,128)S(1)}, u32[]{:S(2)}, u32[]{:S(2)}) collective-permute-start(f32[2,128,512]{1,2,0:T(8,128)S(1)} %bitcast.167), channel_id=1, source_target_pairs={{0,6},{2,8},{4,10},{6,12},{8,14},{1,7},{3,9},{5,11},{7,13},{9,15},... | collective-permute-start | bytes 1572872 | tf_op jit(solution)/shard_map/ppermute | solution.py:16
  169.9 2.3 collective-permute-start.14
  172.2 3.0 %collective-permute-start.13 = (f32[2,128,512]{1,2,0:T(8,128)}, f32[2,128,512]{1,2,0:T(8,128)}, u32[]{:S(2)}, u32[]{:S(2)}) collective-permute-start(f32[2,128,512]{1,2,0:T(8,128)} %bitcast.55), channel_id=1, source_target_pairs={{0,2},{2,4},{4,6},{6,8},{8,10},{10,12},{12,14},{1,3},{3,5},{5,7},{... | collective-permute-start | bytes 1572872 | tf_op jit(solution)/shard_map/ppermute | solution.py:16
  175.2 4.2 %collective-permute-start.12 = (f32[2,128,512]{1,2,0:T(8,128)S(1)}, f32[2,128,512]{1,2,0:T(8,128)}, u32[]{:S(2)}, u32[]{:S(2)}) collective-permute-start(f32[2,128,512]{1,2,0:T(8,128)S(1)} %bitcast.166), channel_id=1, source_target_pairs={{2,0},{4,2},{6,4},{8,6},{10,8},{12,10},{14,12},{3,1},{5,3},{7,5},{... | collective-permute-start | bytes 1572872 | tf_op jit(solution)/shard_map/ppermute | solution.py:16
  179.4 2.7 %collective-permute-start.11 = (f32[2,128,512]{1,2,0:T(8,128)S(1)}, f32[2,128,512]{1,2,0:T(8,128)}, u32[]{:S(2)}, u32[]{:S(2)}) collective-permute-start(f32[2,128,512]{1,2,0:T(8,128)S(1)} %bitcast.165), channel_id=1, source_target_pairs={{4,0},{6,2},{8,4},{10,6},{12,8},{14,10},{5,1},{7,3},{9,5},{11,7},{... | collective-permute-start | bytes 1572872 | tf_op jit(solution)/shard_map/ppermute | solution.py:16
  182.1 6.7 %collective-permute-done.15 = f32[2,128,512]{1,2,0:T(8,128)S(1)} collective-permute-done((f32[2,128,512]{1,2,0:T(8,128)S(1)}, f32[2,128,512]{1,2,0:T(8,128)S(1)}, u32[]{:S(2)}, u32[]{:S(2)}) %collective-permute-start.15) | collective-permute-done | bytes 524320 | tf_op jit(solution)/shard_map/ppermute | solution.py:16
  191.4 9.6 %collective-permute-done.14 = f32[2,128,512]{1,2,0:T(8,128)} collective-permute-done((f32[2,128,512]{1,2,0:T(8,128)}, f32[2,128,512]{1,2,0:T(8,128)}, u32[]{:S(2)}, u32[]{:S(2)}) %collective-permute-start.14) | collective-permute-done | bytes 524320 | tf_op jit(solution)/shard_map/ppermute | solution.py:16
  201.0 18.6 %collective-permute-done.13 = f32[2,128,512]{1,2,0:T(8,128)} collective-permute-done((f32[2,128,512]{1,2,0:T(8,128)}, f32[2,128,512]{1,2,0:T(8,128)}, u32[]{:S(2)}, u32[]{:S(2)}) %collective-permute-start.13) | collective-permute-done | bytes 524320 | tf_op jit(solution)/shard_map/ppermute | solution.py:16
  219.6 2.1 collective-permute-done.11
  225.3 2.4 reduce_sum.339
  227.7 29.4 %all-gather.5.cloned.1.call-done = bf16[512,1024]{1,0:T(8,128)(2,1)} async-done(((bf16[32,1024]{1,0:T(8,128)(2,1)}), bf16[512,1024]{1,0:T(8,128)(2,1)}) %all-gather.5.cloned.1.call-update) | async-done | bytes 1048592 | tf_op jit(solution)/shard_map/all_gather | solution.py:122
  257.1 2.3 copy.82
  (131 shorter events, 48.8 us)
Async XLA Ops:
  7.2 47.9 %copy-start = (bf16[512,1024]{1,0:T(8,128)(2,1)S(1)}, bf16[512,1024]{1,0:T(8,128)(2,1)}, u32[]{:S(2)}) copy-start(bf16[512,1024]{1,0:T(8,128)(2,1)} %param.11) | copy-start | bytes 3145732
  7.2 142.5 %reduce-scatter.2.cloned.1.call-start = ((), (), s32[]{:S(2)}) async-start(), calls=%async_computation.1 | async-start | bytes 2228224 | tf_op jit(solution)/shard_map/reduce_scatter | solution.py:121
  9.1 20.8 %collective-permute-start = (bf16[2,128,512]{2,1,0:T(8,128)(2,1)S(1)}, bf16[2,128,512]{2,1,0:T(8,128)(2,1)S(1)}, u32[]{:S(2)}, u32[]{:S(2)}) collective-permute-start(bf16[2,128,512]{2,1,0:T(8,128)(2,1)S(1)} %constant_dynamic-update-slice_fusion), channel_id=1, source_target_pairs={{0,6},{2,8},{4,10},{6,12},{8,14},{1,7},{3,9},{5,11},{7,13},{9,15},... | collective-permute-start | bytes 786440 | tf_op jit(solution)/shard_map/ppermute | solution.py:16
  13.6 17.7 %collective-permute-start.1 = (bf16[2,128,512]{2,1,0:T(8,128)(2,1)S(1)}, bf16[2,128,512]{2,1,0:T(8,128)(2,1)S(1)}, u32[]{:S(2)}, u32[]{:S(2)}) collective-permute-start(bf16[2,128,512]{2,1,0:T(8,128)(2,1)S(1)} %constant_dynamic-update-slice_fusion), channel_id=1, source_target_pairs={{0,4},{2,6},{4,8},{6,10},{8,12},{10,14},{1,5},{3,7},{5,9},{7,11},{... | collective-permute-start | bytes 786440 | tf_op jit(solution)/shard_map/ppermute | solution.py:16
  17.1 15.3 %collective-permute-start.2 = (bf16[2,128,512]{2,1,0:T(8,128)(2,1)S(1)}, bf16[2,128,512]{2,1,0:T(8,128)(2,1)S(1)}, u32[]{:S(2)}, u32[]{:S(2)}) collective-permute-start(bf16[2,128,512]{2,1,0:T(8,128)(2,1)S(1)} %constant_dynamic-update-slice_fusion), channel_id=1, source_target_pairs={{0,2},{2,4},{4,6},{6,8},{8,10},{10,12},{12,14},{1,3},{3,5},{5,7},{... | collective-permute-start | bytes 786440 | tf_op jit(solution)/shard_map/ppermute | solution.py:16
  19.0 15.0 %collective-permute-start.3 = (bf16[2,128,512]{2,1,0:T(8,128)(2,1)S(1)}, bf16[2,128,512]{2,1,0:T(8,128)(2,1)S(1)}, u32[]{:S(2)}, u32[]{:S(2)}) collective-permute-start(bf16[2,128,512]{2,1,0:T(8,128)(2,1)S(1)} %constant_dynamic-update-slice_fusion), channel_id=1, source_target_pairs={{2,0},{4,2},{6,4},{8,6},{10,8},{12,10},{14,12},{3,1},{5,3},{7,5},{... | collective-permute-start | bytes 786440 | tf_op jit(solution)/shard_map/ppermute | solution.py:16
  23.8 18.4 %collective-permute-start.4 = (bf16[2,128,512]{2,1,0:T(8,128)(2,1)S(1)}, bf16[2,128,512]{2,1,0:T(8,128)(2,1)S(1)}, u32[]{:S(2)}, u32[]{:S(2)}) collective-permute-start(bf16[2,128,512]{2,1,0:T(8,128)(2,1)S(1)} %constant_dynamic-update-slice_fusion), channel_id=1, source_target_pairs={{4,0},{6,2},{8,4},{10,6},{12,8},{14,10},{5,1},{7,3},{9,5},{11,7},{... | collective-permute-start | bytes 786440 | tf_op jit(solution)/shard_map/ppermute | solution.py:16
  30.0 12.3 %collective-permute-start.5 = (bf16[2,128,512]{2,1,0:T(8,128)(2,1)S(1)}, bf16[2,128,512]{2,1,0:T(8,128)(2,1)S(1)}, u32[]{:S(2)}, u32[]{:S(2)}) collective-permute-start(bf16[2,128,512]{2,1,0:T(8,128)(2,1)S(1)} %constant_dynamic-update-slice_fusion), channel_id=1, source_target_pairs={{6,0},{8,2},{10,4},{12,6},{14,8},{7,1},{9,3},{11,5},{13,7},{15,9},... | collective-permute-start | bytes 786440 | tf_op jit(solution)/shard_map/ppermute | solution.py:16
  53.2 17.1 %copy-start.16 = (f32[1,1024]{1,0:T(1,128)S(1)}, f32[1,1024]{1,0:T(1,128)}, u32[]{:S(2)}) copy-start(f32[1,1024]{1,0:T(1,128)} %get-tuple-element.73) | copy-start | bytes 12292
  53.2 17.1 %copy-start.17 = (f32[1,1024]{1,0:T(1,128)S(1)}, f32[1,1024]{1,0:T(1,128)}, u32[]{:S(2)}) copy-start(f32[1,1024]{1,0:T(1,128)} %get-tuple-element.74) | copy-start | bytes 12292
  53.2 17.1 %copy-start.18 = (f32[1,1024]{1,0:T(1,128)S(1)}, f32[1,1024]{1,0:T(1,128)}, u32[]{:S(2)}) copy-start(f32[1,1024]{1,0:T(1,128)} %get-tuple-element.75) | copy-start | bytes 12292
  53.3 17.1 %copy-start.19 = (f32[1,1024]{1,0:T(1,128)S(1)}, f32[1,1024]{1,0:T(1,128)}, u32[]{:S(2)}) copy-start(f32[1,1024]{1,0:T(1,128)} %get-tuple-element.76) | copy-start | bytes 12292
  53.3 17.1 %copy-start.20 = (f32[1,1024]{1,0:T(1,128)S(1)}, f32[1,1024]{1,0:T(1,128)}, u32[]{:S(2)}) copy-start(f32[1,1024]{1,0:T(1,128)} %get-tuple-element.77) | copy-start | bytes 12292
  53.3 17.1 %copy-start.21 = (f32[1,1024]{1,0:T(1,128)S(1)}, f32[1,1024]{1,0:T(1,128)}, u32[]{:S(2)}) copy-start(f32[1,1024]{1,0:T(1,128)} %get-tuple-element.78) | copy-start | bytes 12292
  53.3 17.1 %copy-start.22 = (f32[1,1024]{1,0:T(1,128)S(1)}, f32[1,1024]{1,0:T(1,128)}, u32[]{:S(2)}) copy-start(f32[1,1024]{1,0:T(1,128)} %get-tuple-element.79) | copy-start | bytes 12292
  53.3 17.1 %copy-start.23 = (f32[1,1024]{1,0:T(1,128)S(1)}, f32[1,1024]{1,0:T(1,128)}, u32[]{:S(2)}) copy-start(f32[1,1024]{1,0:T(1,128)} %get-tuple-element.80) | copy-start | bytes 12292
  53.3 17.1 %copy-start.24 = (f32[1,1024]{1,0:T(1,128)S(1)}, f32[1,1024]{1,0:T(1,128)}, u32[]{:S(2)}) copy-start(f32[1,1024]{1,0:T(1,128)} %get-tuple-element.81) | copy-start | bytes 12292
  55.4 11.3 %collective-permute-start.7 = (bf16[15,1024]{1,0:T(8,128)(2,1)S(1)}, bf16[15,1024]{1,0:T(8,128)(2,1)S(1)}, u32[]{:S(2)}, u32[]{:S(2)}) collective-permute-start(bf16[15,1024]{1,0:T(8,128)(2,1)S(1)} %get-tuple-element.66), channel_id=1, source_target_pairs={{2,0},{4,2},{6,4},{8,6},{10,8},{12,10},{14,12},{3,1},{5,3},{7,5},{... | collective-permute-start | bytes 92168 | tf_op jit(solution)/shard_map/ppermute | solution.py:29
  63.6 6.7 %collective-permute-start.6 = (bf16[15,1024]{1,0:T(8,128)(2,1)S(1)}, bf16[15,1024]{1,0:T(8,128)(2,1)S(1)}, u32[]{:S(2)}, u32[]{:S(2)}) collective-permute-start(bf16[15,1024]{1,0:T(8,128)(2,1)S(1)} %get-tuple-element.65), channel_id=1, source_target_pairs={{0,2},{2,4},{4,6},{6,8},{8,10},{10,12},{12,14},{1,3},{3,5},{5,7},{... | collective-permute-start | bytes 92168 | tf_op jit(solution)/shard_map/ppermute | solution.py:27
  66.7 18.8 %copy-start.13 = (bf16[15,1024]{1,0:T(8,128)(2,1)}, bf16[15,1024]{1,0:T(8,128)(2,1)S(1)}, u32[]{:S(2)}) copy-start(bf16[15,1024]{1,0:T(8,128)(2,1)S(1)} %collective-permute-done.7) | copy-start | bytes 92164
  74.6 6.8 %collective-permute-start.9 = (bf16[15,1024]{1,0:T(8,128)(2,1)S(1)}, bf16[15,1024]{1,0:T(8,128)(2,1)S(1)}, u32[]{:S(2)}, u32[]{:S(2)}) collective-permute-start(bf16[15,1024]{1,0:T(8,128)(2,1)S(1)} %get-tuple-element.64), channel_id=1, source_target_pairs={{0,2},{2,4},{4,6},{6,8},{8,10},{10,12},{12,14},{1,3},{3,5},{5,7},{... | collective-permute-start | bytes 92168 | tf_op jit(solution)/shard_map/ppermute | solution.py:27
  76.5 6.4 %collective-permute-start.8 = (bf16[15,1024]{1,0:T(8,128)(2,1)S(1)}, bf16[15,1024]{1,0:T(8,128)(2,1)S(1)}, u32[]{:S(2)}, u32[]{:S(2)}) collective-permute-start(bf16[15,1024]{1,0:T(8,128)(2,1)S(1)} %get-tuple-element.63), channel_id=1, source_target_pairs={{2,0},{4,2},{6,4},{8,6},{10,8},{12,10},{14,12},{3,1},{5,3},{7,5},{... | collective-permute-start | bytes 92168 | tf_op jit(solution)/shard_map/ppermute | solution.py:29
  88.0 137.3 %all-gather.7.cloned.1.call-start = ((), (), s32[]{:S(2)}) async-start(), calls=%async_computation.3 | async-start | bytes 2228224 | tf_op jit(solution)/shard_map/all_gather | solution.py:123
  100.4 156.7 %all-gather.5.cloned.1.call-start = ((), (), s32[]{:S(2)}) async-start(), calls=%async_computation.2 | async-start | bytes 1114112 | tf_op jit(solution)/shard_map/all_gather | solution.py:122
  151.2 38.9 %copy-start.2 = (bf16[8,128,896]{1,2,0:T(8,128)(2,1)S(1)}, bf16[8,128,896]{1,2,0:T(8,128)(2,1)}, u32[]{:S(2)}) copy-start(bf16[8,128,896]{1,2,0:T(8,128)(2,1)} %copy-done.1) | copy-start | bytes 5505028
  151.3 38.9 %copy-start.6 = (bf16[896,8,64]{0,2,1:T(8,128)(2,1)S(1)}, bf16[896,8,64]{0,2,1:T(8,128)(2,1)}, u32[]{:S(2)}) copy-start(bf16[896,8,64]{0,2,1:T(8,128)(2,1)} %copy-done.5) | copy-start | bytes 2752516
  166.4 22.4 %collective-permute-start.15 = (f32[2,128,512]{1,2,0:T(8,128)S(1)}, f32[2,128,512]{1,2,0:T(8,128)S(1)}, u32[]{:S(2)}, u32[]{:S(2)}) collective-permute-start(f32[2,128,512]{1,2,0:T(8,128)S(1)} %bitcast.167), channel_id=1, source_target_pairs={{0,6},{2,8},{4,10},{6,12},{8,14},{1,7},{3,9},{5,11},{7,13},{9,15},... | collective-permute-start | bytes 1572872 | tf_op jit(solution)/shard_map/ppermute | solution.py:16
  169.9 31.1 %collective-permute-start.14 = (f32[2,128,512]{1,2,0:T(8,128)}, f32[2,128,512]{1,2,0:T(8,128)}, u32[]{:S(2)}, u32[]{:S(2)}) collective-permute-start(f32[2,128,512]{1,2,0:T(8,128)} %bitcast.56), channel_id=1, source_target_pairs={{0,4},{2,6},{4,8},{6,10},{8,12},{10,14},{1,5},{3,7},{5,9},{7,11},{... | collective-permute-start | bytes 1572872 | tf_op jit(solution)/shard_map/ppermute | solution.py:16
  172.2 47.5 %collective-permute-start.13 = (f32[2,128,512]{1,2,0:T(8,128)}, f32[2,128,512]{1,2,0:T(8,128)}, u32[]{:S(2)}, u32[]{:S(2)}) collective-permute-start(f32[2,128,512]{1,2,0:T(8,128)} %bitcast.55), channel_id=1, source_target_pairs={{0,2},{2,4},{4,6},{6,8},{8,10},{10,12},{12,14},{1,3},{3,5},{5,7},{... | collective-permute-start | bytes 1572872 | tf_op jit(solution)/shard_map/ppermute | solution.py:16
  175.2 44.4 %collective-permute-start.12 = (f32[2,128,512]{1,2,0:T(8,128)S(1)}, f32[2,128,512]{1,2,0:T(8,128)}, u32[]{:S(2)}, u32[]{:S(2)}) collective-permute-start(f32[2,128,512]{1,2,0:T(8,128)S(1)} %bitcast.166), channel_id=1, source_target_pairs={{2,0},{4,2},{6,4},{8,6},{10,8},{12,10},{14,12},{3,1},{5,3},{7,5},{... | collective-permute-start | bytes 1572872 | tf_op jit(solution)/shard_map/ppermute | solution.py:16
  179.4 42.3 %collective-permute-start.11 = (f32[2,128,512]{1,2,0:T(8,128)S(1)}, f32[2,128,512]{1,2,0:T(8,128)}, u32[]{:S(2)}, u32[]{:S(2)}) collective-permute-start(f32[2,128,512]{1,2,0:T(8,128)S(1)} %bitcast.165), channel_id=1, source_target_pairs={{4,0},{6,2},{8,4},{10,6},{12,8},{14,10},{5,1},{7,3},{9,5},{11,7},{... | collective-permute-start | bytes 1572872 | tf_op jit(solution)/shard_map/ppermute | solution.py:16
  188.8 32.9 %collective-permute-start.10 = (f32[2,128,512]{1,2,0:T(8,128)S(1)}, f32[2,128,512]{1,2,0:T(8,128)}, u32[]{:S(2)}, u32[]{:S(2)}) collective-permute-start(f32[2,128,512]{1,2,0:T(8,128)S(1)} %bitcast.164), channel_id=1, source_target_pairs={{6,0},{8,2},{10,4},{12,6},{14,8},{7,1},{9,3},{11,5},{13,7},{15,9},... | collective-permute-start | bytes 1572872 | tf_op jit(solution)/shard_map/ppermute | solution.py:16
  (21 other events, 193.2 us)
Sparse Core Ops, SparseCore 0:
  88.1 61.5 reduce-scatter.1
  151.8 67.2 all-gather.6
  221.3 35.7 all-gather.4
